TPU v7x, 32 devices: a whole 2x2x4 slice. The times are simulated.
32 devices in a mesh: sec: 4 (over z), blk: 8 (over y, x, core).
Axes of the slice: x: 2, y: 2, z: 4, core: 2. Of those that a mesh axis runs over, the one named last changes fastest.
Arguments:
- receptor: bfloat16 [16384, 1024], P(('sec', 'blk')), may hold values from -6 to 6
- poses: bfloat16 [4096, 1024], P(('sec', 'blk')), may hold values from -6 to 6
- pairs: int32 [8192, 2], P(('sec', 'blk')), may hold values from 0 to 127
- block_complex: int32 [32], replicated, may hold values from 0 to 15, never falling along the last dimension, each value on 1 to 4 neighbouring positions
- w_key: bfloat16 [1024, 1024], P('blk'), may hold values from -0.1875 to 0.1875
- w_value: bfloat16 [1024, 1024], P('blk'), may hold values from -0.1875 to 0.1875
- w_query: bfloat16 [1024, 1024], replicated, may hold values from -0.1875 to 0.1875
- score_weight: float32 [1024], replicated, may hold values from -24 to 24
Outputs:
- pair_loss: float32 [8192], P(('sec', 'blk'))
- pose_grad: bfloat16 [4096, 1024], P(('sec', 'blk'))
- receptor_grad: bfloat16 [16384, 1024], P(('sec', 'blk'))
Inputs may be any that keep to these rules, and one draw needn't show every extreme that they name: `block_complex`: never falls from one block to the next; each complex holds 1 to 4 consecutive blocks, and some complex holds exactly 4. `pairs`: indices among the 128 poses beside the pair's block.
All inputs are finite; a program needn't handle non-finite values.
Results may differ from a plain program's by a relative error of at most 0.014.
Values may be sent and summed in bfloat16 or wider, within the bound.
No kernel may reach another device: no remote copies, remote signals or barrier semaphores. Data moves between devices by JAX's collectives and lax.ppermute only.
A program may use at most 64 MiB of HBM per device.

v0:
```python
import jax
import jax.numpy as jnp
from jax import lax
from jax.sharding import PartitionSpec as P

H = 16
DH = 64
MOSTB = 4
highest = lax.Precision.HIGHEST


def from_behind(value, axis, steps):
    count = lax.axis_size(axis)
    initial, last = (max(0, -steps), min(count, count - steps))
    return lax.ppermute(value, axis, [(source, source + steps) for source in range(initial, last)])


def features(values):
    return jnp.where(values > 0, values + 1.0, jnp.exp(jnp.minimum(values, 0.0)))


def slope(values):
    return jnp.where(values > 0, jnp.ones_like(values), jnp.exp(jnp.minimum(values, 0.0)))


def local_state(key_feat, val_round):
    rows = key_feat.shape[0]
    key_heads = key_feat.reshape(rows, H, DH)
    val_heads = val_round.reshape(rows, H, DH)
    outer = jnp.einsum(
        "thd,the->dhe", key_heads, val_heads, preferred_element_type=jnp.float32
    ).reshape(DH, H * DH)
    norm_row = jnp.sum(key_feat, axis=0, dtype=jnp.float32)
    return jnp.concatenate([outer, norm_row[None, :]], axis=0)


def complex_total(own, block_complex):
    position = lax.axis_index(("sec", "blk"))
    blocks = block_complex.shape[0]
    mine = jnp.take(block_complex, position)
    total = own
    for reach in range(1, MOSTB):
        lower = from_behind(own.astype(jnp.bfloat16), ("sec", "blk"), reach).astype(own.dtype)
        upper = from_behind(own.astype(jnp.bfloat16), ("sec", "blk"), -reach).astype(own.dtype)
        below = jnp.take(block_complex, jnp.maximum(position - reach, 0))
        above = jnp.take(block_complex, jnp.minimum(position + reach, blocks - 1))
        take_lower = jnp.logical_and(position - reach >= 0, below == mine)
        take_upper = jnp.logical_and(position + reach < blocks, above == mine)
        total = total + jnp.where(take_lower, lower, 0.0) + jnp.where(take_upper, upper, 0.0)
    return total


def pose_side(pose_rows, pair_rows, state, w_query, score_weight):
    count = pose_rows.shape[0]
    queries = jnp.dot(pose_rows, w_query, preferred_element_type=jnp.float32)
    query_heads = features(queries).reshape(count, H, DH)
    state_heads = state[:DH].reshape(DH, H, DH)
    norm_heads = state[DH].reshape(H, DH)
    numer = jnp.einsum("phd,dhe->phe", query_heads, state_heads, precision=highest)
    denom = jnp.sum(query_heads * norm_heads[None], axis=2)
    attended = numer / denom[:, :, None]
    weight_heads = score_weight.reshape(H, DH)
    scores = jnp.sum(attended * weight_heads[None], axis=(1, 2))
    better = jnp.take(scores, pair_rows[:, 0])
    worse = jnp.take(scores, pair_rows[:, 1])
    delta = worse - better
    pair_loss = jax.nn.softplus(delta)
    push = jax.nn.sigmoid(delta)
    slots = lax.broadcasted_iota(jnp.int32, (pair_rows.shape[0], count), 1)
    score_grad = jnp.sum(
        jnp.where(slots == pair_rows[:, 1:2], push[:, None], 0.0)
        - jnp.where(slots == pair_rows[:, 0:1], push[:, None], 0.0),
        axis=0,
    )
    attended_grad = score_grad[:, None, None] * weight_heads[None]
    numer_grad = attended_grad / denom[:, :, None]
    denom_grad = -jnp.sum(attended_grad * attended, axis=2) / denom
    outer_grad = jnp.einsum("phd,phe->dhe", query_heads, numer_grad, precision=highest).reshape(
        DH, H * DH
    )
    norm_grad = jnp.sum(query_heads * denom_grad[:, :, None], axis=0).reshape(H * DH)
    pose_state = jnp.concatenate([outer_grad, norm_grad[None, :]], axis=0)
    feat_grad = (
        jnp.einsum("phe,dhe->phd", numer_grad, state_heads, precision=highest)
        + denom_grad[:, :, None] * norm_heads[None]
    )
    query_grad = (feat_grad.reshape(count, H * DH) * slope(queries)).astype(jnp.bfloat16)
    pose_grad = lax.dot_general(
        query_grad, w_query, (((1,), (1,)), ((), ())), preferred_element_type=jnp.float32
    )
    return (pair_loss, pose_grad.astype(jnp.bfloat16), pose_state)


def shards(receptor, poses, pairs, block_complex, w_key, w_value, w_query, score_weight):
    rows = receptor.shape[0]
    width = receptor.shape[1]
    contract = (((1,), (1,)), ((), ()))
    full_key, full_value = (
        lax.all_gather(w_key, "blk", axis=0, tiled=True),
        lax.all_gather(w_value, "blk", axis=0, tiled=True),
    )
    keys = jnp.dot(receptor, full_key, preferred_element_type=jnp.float32)
    values = jnp.dot(receptor, full_value, preferred_element_type=jnp.float32)
    key_feat = features(keys).astype(jnp.bfloat16)
    val_round = values.astype(jnp.bfloat16)
    state = complex_total(local_state(key_feat, val_round), block_complex)
    pair_loss, pose_grad, pose_state = pose_side(poses, pairs, state, w_query, score_weight)
    state_grad = complex_total(pose_state, block_complex).astype(jnp.bfloat16)
    key_heads = key_feat.reshape(rows, H, DH)
    val_heads = val_round.reshape(rows, H, DH)
    grad_heads = state_grad[:DH].reshape(DH, H, DH)
    norm_back = state_grad[DH].astype(jnp.float32).reshape(H, DH)
    feat_grad = (
        jnp.einsum("the,dhe->thd", val_heads, grad_heads, preferred_element_type=jnp.float32)
        + norm_back[None]
    )
    key_grad = (feat_grad.reshape(rows, width) * slope(keys)).astype(jnp.bfloat16)
    value_grad = (
        jnp.einsum("thd,dhe->the", key_heads, grad_heads, preferred_element_type=jnp.float32)
        .reshape(rows, width)
        .astype(jnp.bfloat16)
    )
    total = lax.dot_general(key_grad, full_key, contract, preferred_element_type=jnp.float32)
    total = total + lax.dot_general(
        value_grad, full_value, contract, preferred_element_type=jnp.float32
    )
    return (pair_loss, pose_grad, total.astype(jnp.bfloat16))


def solution(mesh):
    placed = (
        P(("sec", "blk"), None),
        P(("sec", "blk"), None),
        P(("sec", "blk"), None),
        P(),
        P("blk", None),
        P("blk", None),
        P(),
        P(),
    )
    return jax.shard_map(
        shards,
        mesh=mesh,
        in_specs=placed,
        out_specs=(P(("sec", "blk")), P(("sec", "blk"), None), P(("sec", "blk"), None)),
        check_vma=False,
    )
```

profile of v0, /device:TPU:8, one launch (start us, length us, event | category | flops | bytes accessed | tf_op | source)
XLA Modules:
  0.0 189.3 jit_solution(2240963160841617710)
XLA Ops:
  10.6 2.4 %add_select_fusion = (f32[128,1024]{1,0:T(8,128)}, f32[128,1024]{1,0:T(8,128)}) fusion(bf16[128,1024]{1,0:T(8,128)(2,1)} %param.11, bf16[1024,1024]{1,0:T(8,128)(2,1)S(1)} %copy-done), kind=kOutput, calls=%fused_computation.27 | convolution fusion | flops 268959744 | bytes 3407872 | tf_op jit(solution)/shard_map/dot_general | solution.py:55
  13.0 26.0 %all-gather.3.cloned.1.call-done = bf16[1024,1024]{1,0:T(8,128)(2,1)} async-done(((bf16[128,1024]{1,0:T(8,128)(2,1)}), bf16[1024,1024]{1,0:T(8,128)(2,1)}) %all-gather.3.cloned.1.call-update) | async-done | bytes 2097168 | tf_op jit(solution)/shard_map/all_gather | solution.py:100
  39.0 4.1 %convolution_convert_fusion.1 = bf16[512,1024]{1,0:T(8,128)(2,1)} fusion(bf16[512,1024]{1,0:T(8,128)(2,1)} %param.10, bf16[1024,1024]{1,0:T(8,128)(2,1)} %all-gather.3.cloned.1.call-done), kind=kOutput, calls=%fused_computation.9 | convolution fusion | flops 1074266112 | bytes 4194304 | tf_op jit(solution)/shard_map/dot_general | solution.py:103
  44.6 24.2 %all-gather.5.cloned.1.call-done = bf16[1024,1024]{1,0:T(8,128)(2,1)} async-done(((bf16[128,1024]{1,0:T(8,128)(2,1)}), bf16[1024,1024]{1,0:T(8,128)(2,1)}) %all-gather.5.cloned.1.call-update) | async-done | bytes 2097168 | tf_op jit(solution)/shard_map/all_gather | solution.py:99
  68.8 5.0 %convert_reduce_fusion = (f32[1024]{0:T(1024)S(1)}, bf16[512,1024]{1,0:T(8,128)(2,1)}, f32[512,1024]{1,0:T(8,128)}) fusion(bf16[512,1024]{1,0:T(8,128)(2,1)} %param.10, bf16[1024,1024]{1,0:T(8,128)(2,1)} %all-gather.5.cloned.1.call-done), kind=kOutput, calls=%fused_computation.4 | convolution fusion | flops 1077410816 | bytes 6295552 | tf_op jit(solution)/shard_map/dot_general | solution.py:102
  73.8 2.3 %copy.36 = bf16[512,1024]{0,1:T(8,128)(2,1)} copy(bf16[512,1024]{1,0:T(8,128)(2,1)} %get-tuple-element.84) | data formatting | bytes 2097152 | tf_op jit(solution)/shard_map/convert_element_type | solution.py:104
  76.1 2.4 %fusion.26 = f32[16,64,64]{2,1,0:T(8,128)} fusion(bf16[512,16,64]{0,2,1:T(8,128)(2,1)S(1)} %bitcast.65, bf16[512,16,64]{0,2,1:T(8,128)(2,1)} %bitcast.67), kind=kOutput, calls=%fused_computation.66 | convolution fusion | flops 67108864 | bytes 2359296 | tf_op jit(solution)/shard_map/thd,the->dhe/dot_general | solution.py:30
  80.4 3.1 %collective-permute-start.5 = (bf16[65,1024]{1,0:T(8,128)(2,1)}, bf16[65,1024]{1,0:T(8,128)(2,1)S(1)}, u32[]{:S(2)}, u32[]{:S(2)}) collective-permute-start(bf16[65,1024]{1,0:T(8,128)(2,1)} %fusion.16), channel_id=1, source_target_pairs={{3,0},{4,1},{5,2},{6,3},{7,4},{8,5},{9,6},{10,7},{11,8},{12,9},{13... | collective-permute-start | bytes 399368 | tf_op jit(solution)/shard_map/ppermute | solution.py:15
  84.2 2.4 %collective-permute-start.4 = (bf16[65,1024]{1,0:T(8,128)(2,1)}, bf16[65,1024]{1,0:T(8,128)(2,1)}, u32[]{:S(2)}, u32[]{:S(2)}) collective-permute-start(bf16[65,1024]{1,0:T(8,128)(2,1)} %fusion.16), channel_id=1, source_target_pairs={{0,3},{1,4},{2,5},{3,6},{4,7},{5,8},{6,9},{7,10},{8,11},{9,12},{10... | collective-permute-start | bytes 399368 | tf_op jit(solution)/shard_map/ppermute | solution.py:15
  86.7 5.1 %collective-permute-start.3 = (bf16[65,1024]{1,0:T(8,128)(2,1)}, bf16[65,1024]{1,0:T(8,128)(2,1)}, u32[]{:S(2)}, u32[]{:S(2)}) collective-permute-start(bf16[65,1024]{1,0:T(8,128)(2,1)} %fusion.16), channel_id=1, source_target_pairs={{2,0},{3,1},{4,2},{5,3},{6,4},{7,5},{8,6},{9,7},{10,8},{11,9},{12,... | collective-permute-start | bytes 399368 | tf_op jit(solution)/shard_map/ppermute | solution.py:15
  93.8 4.1 %collective-permute-start.1 = (bf16[65,1024]{1,0:T(8,128)(2,1)}, bf16[65,1024]{1,0:T(8,128)(2,1)}, u32[]{:S(2)}, u32[]{:S(2)}) collective-permute-start(bf16[65,1024]{1,0:T(8,128)(2,1)} %fusion.16), channel_id=1, source_target_pairs={{1,0},{2,1},{3,2},{4,3},{5,4},{6,5},{7,6},{8,7},{9,8},{10,9},{11,1... | collective-permute-start | bytes 399368 | tf_op jit(solution)/shard_map/ppermute | solution.py:15
  115.1 2.7 %multiply_reduce_fusion.1 = (f32[128]{0:T(128)S(1)}, f32[128,16,64]{0,2,1:T(8,128)}) fusion(f32[16,64]{1,0:T(8,128)} %mul.68, f32[128,16]{0,1:T(8,128)S(1)} %multiply_reduce_fusion.2, f32[64,16,64]{0,2,1:T(8,128)} %bitcast.77, f32[128,16,64]{0,2,1:T(8,128)} %bitcast.73), kind=kOutput, calls=%fused_computation.24 | convolution fusion | flops 101056384 | bytes 1323520 | tf_op jit(solution)/shard_map/phd,dhe->phe/dot_general | solution.py:59
  122.6 2.9 %fusion.6 = f32[16,64,64]{2,1,0:T(8,128)} fusion(f32[128,16,64]{0,2,1:T(8,128)} %bitcast.74, f32[128]{0:T(128)S(1)} %subtract_reduce_fusion, f32[16,64]{1,0:T(8,128)S(1)} %copy-done.6, f32[128,16]{0,1:T(8,128)S(1)} %multiply_reduce_fusion.2), kind=kOutput, calls=%fused_computation.28 | convolution fusion | flops 100925440 | bytes 799232 | tf_op jit(solution)/shard_map/phd,phe->dhe/dot_general | solution.py:78
  134.5 3.8 %collective-permute-start.11 = (bf16[65,1024]{1,0:T(8,128)(2,1)}, bf16[65,1024]{1,0:T(8,128)(2,1)S(1)}, u32[]{:S(2)}, u32[]{:S(2)}) collective-permute-start(bf16[65,1024]{1,0:T(8,128)(2,1)} %fusion.15), channel_id=1, source_target_pairs={{3,0},{4,1},{5,2},{6,3},{7,4},{8,5},{9,6},{10,7},{11,8},{12,9},{13... | collective-permute-start | bytes 399368 | tf_op jit(solution)/shard_map/ppermute | solution.py:15
  140.2 5.7 %collective-permute-start.9 = (bf16[65,1024]{1,0:T(8,128)(2,1)}, bf16[65,1024]{1,0:T(8,128)(2,1)}, u32[]{:S(2)}, u32[]{:S(2)}) collective-permute-start(bf16[65,1024]{1,0:T(8,128)(2,1)} %fusion.15), channel_id=1, source_target_pairs={{2,0},{3,1},{4,2},{5,3},{6,4},{7,5},{8,6},{9,7},{10,8},{11,9},{12,... | collective-permute-start | bytes 399368 | tf_op jit(solution)/shard_map/ppermute | solution.py:15
  147.8 5.7 %collective-permute-start.7 = (bf16[65,1024]{1,0:T(8,128)(2,1)}, bf16[65,1024]{1,0:T(8,128)(2,1)}, u32[]{:S(2)}, u32[]{:S(2)}) collective-permute-start(bf16[65,1024]{1,0:T(8,128)(2,1)} %fusion.15), channel_id=1, source_target_pairs={{1,0},{2,1},{3,2},{4,3},{5,4},{6,5},{7,6},{8,7},{9,8},{10,9},{11,1... | collective-permute-start | bytes 399368 | tf_op jit(solution)/shard_map/ppermute | solution.py:15
  153.5 2.1 %copy.41 = f32[128,1024]{1,0:T(8,128)} copy(f32[128,1024]{0,1:T(8,128)} %bitcast.80) | data formatting | bytes 1048576 | tf_op jit(solution)/shard_map/reshape | solution.py:87
  155.6 2.7 %convolution_convert_fusion.2 = bf16[128,1024]{1,0:T(8,128)(2,1)} fusion(bf16[1024,1024]{1,0:T(8,128)(2,1)S(1)} %copy-done, f32[128,1024]{1,0:T(8,128)} %copy.41, f32[128,1024]{1,0:T(8,128)} %get-tuple-element.96), kind=kOutput, calls=%fused_computation.14 | convolution fusion | flops 269221888 | bytes 3407872 | tf_op jit(solution)/shard_map/dot_general | solution.py:88
  158.3 2.1 %collective-permute-start.6 = (bf16[65,1024]{1,0:T(8,128)(2,1)}, bf16[65,1024]{1,0:T(8,128)(2,1)S(1)}, u32[]{:S(2)}, u32[]{:S(2)}) collective-permute-start(bf16[65,1024]{1,0:T(8,128)(2,1)} %fusion.15), channel_id=1, source_target_pairs={{0,1},{1,2},{2,3},{3,4},{4,5},{5,6},{6,7},{7,8},{8,9},{9,10},{10,1... | collective-permute-start | bytes 399368 | tf_op jit(solution)/shard_map/ppermute | solution.py:15
  161.0 5.7 %collective-permute-done.6 = bf16[65,1024]{1,0:T(8,128)(2,1)S(1)} collective-permute-done((bf16[65,1024]{1,0:T(8,128)(2,1)}, bf16[65,1024]{1,0:T(8,128)(2,1)S(1)}, u32[]{:S(2)}, u32[]{:S(2)}) %collective-permute-start.6) | collective-permute-done | bytes 133152 | tf_op jit(solution)/shard_map/ppermute | solution.py:15
  168.4 2.6 %convolution_convert_fusion = bf16[16,64,512]{2,1,0:T(8,128)(2,1)} fusion(bf16[64,16,64]{0,2,1:T(8,128)(2,1)S(1)} %bitcast.70, bf16[512,16,64]{0,2,1:T(8,128)(2,1)} %bitcast.68), kind=kOutput, calls=%fused_computation.8 | convolution fusion | flops 67633152 | bytes 2228224 | tf_op jit(solution)/shard_map/thd,dhe->the/dot_general | solution.py:119
  172.9 2.9 %copy.45 = f32[512,1024]{1,0:T(8,128)} copy(f32[512,1024]{0,1:T(8,128)} %bitcast.69) | data formatting | bytes 4194304 | tf_op jit(solution)/shard_map/reshape | solution.py:117
  175.8 4.3 %fusion.2 = f32[512,1024]{1,0:T(8,128)S(1)} fusion(bf16[1024,1024]{1,0:T(8,128)(2,1)} %all-gather.5.cloned.1.call-done, f32[512,1024]{1,0:T(8,128)} %copy.45, f32[512,1024]{1,0:T(8,128)} %get-tuple-element.94), kind=kOutput, calls=%fused_computation.15 | convolution fusion | flops 1076363264 | bytes 8388608 | tf_op jit(solution)/shard_map/dot_general | solution.py:123
  180.1 2.3 %add_convert_fusion = bf16[512,1024]{1,0:T(8,128)(2,1)} fusion(f32[512,1024]{1,0:T(8,128)S(1)} %fusion.2, bf16[512,1024]{0,1:T(8,128)(2,1)S(1)} %bitcast.76, bf16[1024,1024]{1,0:T(8,128)(2,1)S(1)} %copy-done.12), kind=kOutput, calls=%fused_computation.2 | convolution fusion | flops 1074790400 | bytes 6291456 | tf_op jit(solution)/shard_map/dot_general | solution.py:124
  (81 shorter events, 43.6 us)
Async XLA Ops:
  7.2 31.8 %all-gather.3.cloned.1.call-start = ((), (), s32[]{:S(2)}) async-start(), calls=%async_computation | async-start | bytes 2359296 | tf_op jit(solution)/shard_map/all_gather | solution.py:100
  7.9 60.9 %all-gather.5.cloned.1.call-start = ((), (), s32[]{:S(2)}) async-start(), calls=%async_computation.1 | async-start | bytes 2359296 | tf_op jit(solution)/shard_map/all_gather | solution.py:99
  10.0 29.0 %copy-start.9 = (s32[256,1]{0,1:T(1,128)}, s32[256,1]{0,1:T(1,128)S(1)}, u32[]{:S(2)}) copy-start(s32[256,1]{0,1:T(1,128)S(1)} %get-tuple-element.86) | copy-start | bytes 3076
  73.8 5.9 %copy-start.7 = (f32[1024]{0:T(1024)}, f32[1024]{0:T(1024)S(1)}, u32[]{:S(2)}) copy-start(f32[1024]{0:T(1024)S(1)} %get-tuple-element.83) | copy-start | bytes 12292
  80.4 17.5 %collective-permute-start.5 = (bf16[65,1024]{1,0:T(8,128)(2,1)}, bf16[65,1024]{1,0:T(8,128)(2,1)S(1)}, u32[]{:S(2)}, u32[]{:S(2)}) collective-permute-start(bf16[65,1024]{1,0:T(8,128)(2,1)} %fusion.16), channel_id=1, source_target_pairs={{3,0},{4,1},{5,2},{6,3},{7,4},{8,5},{9,6},{10,7},{11,8},{12,9},{13... | collective-permute-start | bytes 399368 | tf_op jit(solution)/shard_map/ppermute | solution.py:15
  84.2 27.0 %collective-permute-start.4 = (bf16[65,1024]{1,0:T(8,128)(2,1)}, bf16[65,1024]{1,0:T(8,128)(2,1)}, u32[]{:S(2)}, u32[]{:S(2)}) collective-permute-start(bf16[65,1024]{1,0:T(8,128)(2,1)} %fusion.16), channel_id=1, source_target_pairs={{0,3},{1,4},{2,5},{3,6},{4,7},{5,8},{6,9},{7,10},{8,11},{9,12},{10... | collective-permute-start | bytes 399368 | tf_op jit(solution)/shard_map/ppermute | solution.py:15
  86.7 24.5 %collective-permute-start.3 = (bf16[65,1024]{1,0:T(8,128)(2,1)}, bf16[65,1024]{1,0:T(8,128)(2,1)}, u32[]{:S(2)}, u32[]{:S(2)}) collective-permute-start(bf16[65,1024]{1,0:T(8,128)(2,1)} %fusion.16), channel_id=1, source_target_pairs={{2,0},{3,1},{4,2},{5,3},{6,4},{7,5},{8,6},{9,7},{10,8},{11,9},{12,... | collective-permute-start | bytes 399368 | tf_op jit(solution)/shard_map/ppermute | solution.py:15
  91.8 19.4 %collective-permute-start.2 = (bf16[65,1024]{1,0:T(8,128)(2,1)}, bf16[65,1024]{1,0:T(8,128)(2,1)}, u32[]{:S(2)}, u32[]{:S(2)}) collective-permute-start(bf16[65,1024]{1,0:T(8,128)(2,1)} %fusion.16), channel_id=1, source_target_pairs={{0,2},{1,3},{2,4},{3,5},{4,6},{5,7},{6,8},{7,9},{8,10},{9,11},{10,... | collective-permute-start | bytes 399368 | tf_op jit(solution)/shard_map/ppermute | solution.py:15
  93.8 17.5 %collective-permute-start.1 = (bf16[65,1024]{1,0:T(8,128)(2,1)}, bf16[65,1024]{1,0:T(8,128)(2,1)}, u32[]{:S(2)}, u32[]{:S(2)}) collective-permute-start(bf16[65,1024]{1,0:T(8,128)(2,1)} %fusion.16), channel_id=1, source_target_pairs={{1,0},{2,1},{3,2},{4,3},{5,4},{6,5},{7,6},{8,7},{9,8},{10,9},{11,1... | collective-permute-start | bytes 399368 | tf_op jit(solution)/shard_map/ppermute | solution.py:15
  97.9 13.3 %collective-permute-start = (bf16[65,1024]{1,0:T(8,128)(2,1)}, bf16[65,1024]{1,0:T(8,128)(2,1)}, u32[]{:S(2)}, u32[]{:S(2)}) collective-permute-start(bf16[65,1024]{1,0:T(8,128)(2,1)} %fusion.16), channel_id=1, source_target_pairs={{0,1},{1,2},{2,3},{3,4},{4,5},{5,6},{6,7},{7,8},{8,9},{9,10},{10,1... | collective-permute-start | bytes 399368 | tf_op jit(solution)/shard_map/ppermute | solution.py:15
  115.0 6.8 %copy-start.8 = (s32[256,1]{0,1:T(1,128)S(1)}, s32[256,1]{0,1:T(1,128)}, u32[]{:S(2)}) copy-start(s32[256,1]{0,1:T(1,128)} %get-tuple-element.85) | copy-start | bytes 3076
  115.1 6.8 %copy-start.10 = (s32[256,1]{0,1:T(1,128)S(1)}, s32[256,1]{0,1:T(1,128)}, u32[]{:S(2)}) copy-start(s32[256,1]{0,1:T(1,128)} %copy-done.9) | copy-start | bytes 3076
  115.1 7.5 %copy-start.6 = (f32[16,64]{1,0:T(8,128)S(1)}, f32[16,64]{1,0:T(8,128)}, u32[]{:S(2)}) copy-start(f32[16,64]{1,0:T(8,128)} %mul.68) | copy-start | bytes 12292
  121.8 3.9 %copy-start.2 = (f32[64,1024]{0,1:T(8,128)S(1)}, f32[64,1024]{0,1:T(8,128)}, u32[]{:S(2)}) copy-start(f32[64,1024]{0,1:T(8,128)} %copy.38) | copy-start | bytes 786436
  134.5 23.8 %collective-permute-start.11 = (bf16[65,1024]{1,0:T(8,128)(2,1)}, bf16[65,1024]{1,0:T(8,128)(2,1)S(1)}, u32[]{:S(2)}, u32[]{:S(2)}) collective-permute-start(bf16[65,1024]{1,0:T(8,128)(2,1)} %fusion.15), channel_id=1, source_target_pairs={{3,0},{4,1},{5,2},{6,3},{7,4},{8,5},{9,6},{10,7},{11,8},{12,9},{13... | collective-permute-start | bytes 399368 | tf_op jit(solution)/shard_map/ppermute | solution.py:15
  138.3 22.8 %collective-permute-start.10 = (bf16[65,1024]{1,0:T(8,128)(2,1)}, bf16[65,1024]{1,0:T(8,128)(2,1)}, u32[]{:S(2)}, u32[]{:S(2)}) collective-permute-start(bf16[65,1024]{1,0:T(8,128)(2,1)} %fusion.15), channel_id=1, source_target_pairs={{0,3},{1,4},{2,5},{3,6},{4,7},{5,8},{6,9},{7,10},{8,11},{9,12},{10... | collective-permute-start | bytes 399368 | tf_op jit(solution)/shard_map/ppermute | solution.py:15
  140.2 20.8 %collective-permute-start.9 = (bf16[65,1024]{1,0:T(8,128)(2,1)}, bf16[65,1024]{1,0:T(8,128)(2,1)}, u32[]{:S(2)}, u32[]{:S(2)}) collective-permute-start(bf16[65,1024]{1,0:T(8,128)(2,1)} %fusion.15), channel_id=1, source_target_pairs={{2,0},{3,1},{4,2},{5,3},{6,4},{7,5},{8,6},{9,7},{10,8},{11,9},{12,... | collective-permute-start | bytes 399368 | tf_op jit(solution)/shard_map/ppermute | solution.py:15
  145.9 15.2 %collective-permute-start.8 = (bf16[65,1024]{1,0:T(8,128)(2,1)}, bf16[65,1024]{1,0:T(8,128)(2,1)}, u32[]{:S(2)}, u32[]{:S(2)}) collective-permute-start(bf16[65,1024]{1,0:T(8,128)(2,1)} %fusion.15), channel_id=1, source_target_pairs={{0,2},{1,3},{2,4},{3,5},{4,6},{5,7},{6,8},{7,9},{8,10},{9,11},{10,... | collective-permute-start | bytes 399368 | tf_op jit(solution)/shard_map/ppermute | solution.py:15
  147.8 13.2 %collective-permute-start.7 = (bf16[65,1024]{1,0:T(8,128)(2,1)}, bf16[65,1024]{1,0:T(8,128)(2,1)}, u32[]{:S(2)}, u32[]{:S(2)}) collective-permute-start(bf16[65,1024]{1,0:T(8,128)(2,1)} %fusion.15), channel_id=1, source_target_pairs={{1,0},{2,1},{3,2},{4,3},{5,4},{6,5},{7,6},{8,7},{9,8},{10,9},{11,1... | collective-permute-start | bytes 399368 | tf_op jit(solution)/shard_map/ppermute | solution.py:15
  155.6 4.9 %copy-start.11 = (f32[256]{0:T(256)S(1)}, f32[256]{0:T(256)}, u32[]{:S(2)}) copy-start(f32[256]{0:T(256)} %get-tuple-element.82) | copy-start | bytes 3076
  155.6 11.2 %copy-start.5 = (f32[1024]{0:T(1024)S(1)}, f32[1024]{0:T(1024)}, u32[]{:S(2)}) copy-start(f32[1024]{0:T(1024)} %copy-done.4) | copy-start | bytes 12292
  158.3 8.5 %collective-permute-start.6 = (bf16[65,1024]{1,0:T(8,128)(2,1)}, bf16[65,1024]{1,0:T(8,128)(2,1)S(1)}, u32[]{:S(2)}, u32[]{:S(2)}) collective-permute-start(bf16[65,1024]{1,0:T(8,128)(2,1)} %fusion.15), channel_id=1, source_target_pairs={{0,1},{1,2},{2,3},{3,4},{4,5},{5,6},{6,7},{7,8},{8,9},{9,10},{10,1... | collective-permute-start | bytes 399368 | tf_op jit(solution)/shard_map/ppermute | solution.py:15
  175.8 4.3 %copy-start.1 = (bf16[16,64,512]{2,1,0:T(8,128)(2,1)S(1)}, bf16[16,64,512]{2,1,0:T(8,128)(2,1)}, u32[]{:S(2)}) copy-start(bf16[16,64,512]{2,1,0:T(8,128)(2,1)} %convolution_convert_fusion) | copy-start | bytes 3145732
  175.8 4.3 %copy-start.12 = (bf16[1024,1024]{1,0:T(8,128)(2,1)S(1)}, bf16[1024,1024]{1,0:T(8,128)(2,1)}, u32[]{:S(2)}) copy-start(bf16[1024,1024]{1,0:T(8,128)(2,1)} %all-gather.3.cloned.1.call-done) | copy-start | bytes 6291460
  (3 other events, 7.7 us)
Sparse Core Ops, SparseCore 0:
  9.9 29.0 all-gather.2
  40.9 27.8 all-gather.4
where the time goes:
time: 190 us; the launch traced here: 189 us
  waiting for transfers between devices  57.3 us (30%)
  starting transfers between devices  39.8 us (21%)
  matrix products  35.4 us (19%)
  local copies, waits for them, and re-layouts  26.5 us (14%)
  between operations  18.9 us (10%)
  other arithmetic  11.4 us (6%)
    ppermute x12, starting transfers between devices, from_behind(): lax.ppermute(value, axis, [(source, source + steps) for source in range(i...  39.7 us
    all_gather x1, waiting for transfers between devices, shards(): lax.all_gather(w_value, 'blk', axis=0, tiled=True)  26 us
    all_gather x1, waiting for transfers between devices, shards(): lax.all_gather(w_key, 'blk', axis=0, tiled=True)  24.2 us
    ppermute x12, waiting for transfers between devices, from_behind(): lax.ppermute(value, axis, [(source, source + steps) for source in range(i...  5.78 us
    dot_general x1, matrix products, shards(): keys = jnp.dot(receptor, full_key, preferred_element_type=jnp.float32)  5.01 us
    dot_general x1, matrix products, shards(): lax.dot_general(key_grad, full_key, contract, preferred_element_type=jnp....  4.29 us
    dot_general x1, matrix products, shards(): values = jnp.dot(receptor, full_value, preferred_element_type=jnp.float32)  4.14 us
  transfers between devices with their start and end apart: 14, of which 3 were waited for; matrix products, arithmetic and copies ran while one was open for 12% of the time, Pallas kernels for 0%

commit v1 on v0

--- a/solution.py
+++ b/solution.py
@@ -7,6 +7,27 @@
 DH = 64
 MOSTB = 4
 highest = lax.Precision.HIGHEST
+
+
+def gather_around(x, axis, dim):
+    size, place, rows = (lax.axis_size(axis), lax.axis_index(axis), x.shape[dim])
+    right = [(i, (i + 1) % size) for i in range(size)]
+    behind = [(i, (i - 1) % size) for i in range(size)]
+    result = jnp.zeros((*x.shape[:dim], size * rows, *x.shape[dim + 1 :]), x.dtype)
+    result = lax.dynamic_update_slice_in_dim(result, x, place * rows, axis=dim)
+    from_left = from_right = x
+    halfway = size // 2
+    for step in range(1, halfway + 1):
+        from_left = lax.ppermute(from_left, axis, right)
+        result = lax.dynamic_update_slice_in_dim(
+            result, from_left, (place - step) % size * rows, axis=dim
+        )
+        if step < size - halfway:
+            from_right = lax.ppermute(from_right, axis, behind)
+            result = lax.dynamic_update_slice_in_dim(
+                result, from_right, (place + step) % size * rows, axis=dim
+            )
+    return result
 
 
 def from_behind(value, axis, steps):
@@ -96,7 +117,7 @@
     width = receptor.shape[1]
     contract = (((1,), (1,)), ((), ()))
     full_key, full_value = (
-        lax.all_gather(w_key, "blk", axis=0, tiled=True),
+        gather_around(w_key, "blk", 0),
         lax.all_gather(w_value, "blk", axis=0, tiled=True),
     )
     keys = jnp.dot(receptor, full_key, preferred_element_type=jnp.float32)

time: 190 us -> 169 us (0.89)
  waiting for transfers between devices: 57.3 us -> 30 us
  starting transfers between devices: 39.8 us -> 45.9 us
  matrix products: 35.4 us -> 31.2 us
  local copies, waits for them, and re-layouts: 26.5 us -> 29.9 us
    all_gather x1, waiting for transfers between devices: 26 us -> 0.01 us  [shards(): lax.all_gather(w_value, 'blk', axis=0, tiled=True)]
    all_gather x1 -> x0, waiting for transfers between devices: 24.2 us -> none  [shards(): lax.all_gather(w_key, 'blk', axis=0, tiled=True)]
    ppermute x0 -> x7, waiting for transfers between devices: none -> 23.3 us  [the longest x4 22.7 us: gather_around(): from_left = lax.ppermute(from_left, axis, right)]
    ppermute x0 -> x7, starting transfers between devices: none -> 7.24 us  [the longest x3 7.23 us: gather_around(): from_right = lax.ppermute(from_right, axis, behind)]
    dynamic_update_slice x0 -> x8, local copies, waits for them, and re-layouts: none -> 5.76 us  [the longest x4 2.85 us: gather_around(): lax.dynamic_update_slice_in_dim(result, from_left, (place - step) % size...]
    reshape x1 -> x0, local copies, waits for them, and re-layouts: 2.92 us -> none  [shards(): feat_grad.reshape(rows, width) * slope(keys)]
    convert_element_type x1 -> x0, local copies, waits for them, and re-layouts: 2.27 us -> none  [shards(): key_feat = features(keys).astype(jnp.bfloat16)]
    unnamed x26 -> x32, local copies, waits for them, and re-layouts: 0.64 us -> 2.75 us
  transfers between devices with their start and end apart: 14 -> 20, of which waited for: 3 -> 6; matrix products, arithmetic and copies ran while one was open for 12% -> 17% of each run, Pallas kernels for 0% -> 0%
where the time goes in v1:
time: 169 us; the launch traced here: 168 us
  starting transfers between devices  45.9 us (27%)
  matrix products  31.2 us (18%)
  waiting for transfers between devices  30 us (18%)
  local copies, waits for them, and re-layouts  29.9 us (18%)
  between operations  18.9 us (11%)
  other arithmetic  11.9 us (7%)
    ppermute x12, starting transfers between devices, from_behind(): lax.ppermute(value, axis, [(source, source + steps) for source in range(i...  38.6 us
    ppermute x4, waiting for transfers between devices, gather_around(): from_left = lax.ppermute(from_left, axis, right)  22.7 us
    ppermute x3, starting transfers between devices, gather_around(): from_right = lax.ppermute(from_right, axis, behind)  7.23 us
    ppermute x12, waiting for transfers between devices, from_behind(): lax.ppermute(value, axis, [(source, source + steps) for source in range(i...  5.96 us
    dot_general x1, matrix products, shards(): keys = jnp.dot(receptor, full_key, preferred_element_type=jnp.float32)  4.87 us
    dot_general x1, matrix products, shards(): lax.dot_general(key_grad, full_key, contract, preferred_element_type=jnp....  3.88 us
    dot_general x1, matrix products, shards(): values = jnp.dot(receptor, full_value, preferred_element_type=jnp.float32)  3.82 us
  transfers between devices with their start and end apart: 20, of which 6 were waited for; matrix products, arithmetic and copies ran while one was open for 17% of the time, Pallas kernels for 0%

profile of v1, /device:TPU:8, one launch (start us, length us, event | category | flops | bytes accessed | tf_op | source)
XLA Modules:
  0.0 167.9 jit_solution(8671224017854241674)
XLA Ops:
  9.9 2.5 %add_select_fusion = (f32[128,1024]{1,0:T(8,128)}, f32[128,1024]{1,0:T(8,128)}) fusion(bf16[128,1024]{1,0:T(8,128)(2,1)} %param.11, bf16[1024,1024]{1,0:T(8,128)(2,1)S(1)} %copy-done), kind=kOutput, calls=%fused_computation.25 | convolution fusion | flops 268959744 | bytes 3407872 | tf_op jit(solution)/shard_map/dot_general | solution.py:76
  12.3 5.5 %collective-permute-done = bf16[128,1024]{1,0:T(8,128)(2,1)S(1)} collective-permute-done((bf16[128,1024]{1,0:T(8,128)(2,1)}, bf16[128,1024]{1,0:T(8,128)(2,1)S(1)}, u32[]{:S(2)}, u32[]{:S(2)}) %collective-permute-start) | collective-permute-done | bytes 262176 | tf_op jit(solution)/shard_map/ppermute | solution.py:21
  18.4 2.6 %collective-permute-start.3 = (bf16[128,1024]{1,0:T(8,128)(2,1)S(1)}, bf16[128,1024]{1,0:T(8,128)(2,1)S(1)}, u32[]{:S(2)}, u32[]{:S(2)}) collective-permute-start(bf16[128,1024]{1,0:T(8,128)(2,1)S(1)} %collective-permute-done.1), channel_id=1, source_target_pairs={{0,7},{1,0},{2,1},{3,2},{4,3},{5,4},{6,5},{7,6},{8,15},{9,8},{10,9... | collective-permute-start | bytes 786440 | tf_op jit(solution)/shard_map/ppermute | solution.py:26
  23.4 6.2 %collective-permute-done.2 = bf16[128,1024]{1,0:T(8,128)(2,1)S(1)} collective-permute-done((bf16[128,1024]{1,0:T(8,128)(2,1)S(1)}, bf16[128,1024]{1,0:T(8,128)(2,1)S(1)}, u32[]{:S(2)}, u32[]{:S(2)}) %collective-permute-start.2) | collective-permute-done | bytes 262176 | tf_op jit(solution)/shard_map/ppermute | solution.py:21
  31.1 2.6 %collective-permute-start.5 = (bf16[128,1024]{1,0:T(8,128)(2,1)S(1)}, bf16[128,1024]{1,0:T(8,128)(2,1)S(1)}, u32[]{:S(2)}, u32[]{:S(2)}) collective-permute-start(bf16[128,1024]{1,0:T(8,128)(2,1)S(1)} %collective-permute-done.3), channel_id=1, source_target_pairs={{0,7},{1,0},{2,1},{3,2},{4,3},{5,4},{6,5},{7,6},{8,15},{9,8},{10,9... | collective-permute-start | bytes 786440 | tf_op jit(solution)/shard_map/ppermute | solution.py:26
  34.4 7.1 %collective-permute-done.4 = bf16[128,1024]{1,0:T(8,128)(2,1)S(1)} collective-permute-done((bf16[128,1024]{1,0:T(8,128)(2,1)S(1)}, bf16[128,1024]{1,0:T(8,128)(2,1)S(1)}, u32[]{:S(2)}, u32[]{:S(2)}) %collective-permute-start.4) | collective-permute-done | bytes 262176 | tf_op jit(solution)/shard_map/ppermute | solution.py:21
  44.3 3.9 %collective-permute-done.6 = bf16[128,1024]{1,0:T(8,128)(2,1)S(1)} collective-permute-done((bf16[128,1024]{1,0:T(8,128)(2,1)S(1)}, bf16[128,1024]{1,0:T(8,128)(2,1)S(1)}, u32[]{:S(2)}, u32[]{:S(2)}) %collective-permute-start.6) | collective-permute-done | bytes 262176 | tf_op jit(solution)/shard_map/ppermute | solution.py:21
  49.0 4.9 %convert_reduce_fusion = (f32[1024]{0:T(1024)S(1)}, bf16[1024,512]{1,0:T(8,128)(2,1)}, f32[1024,512]{1,0:T(8,128)}) fusion(bf16[1024,1024]{1,0:T(8,128)(2,1)} %constant_dynamic-update-slice_fusion, bf16[512,1024]{1,0:T(8,128)(2,1)S(1)} %copy-done.14), kind=kOutput, calls=%fused_computation.5 | convolution fusion | flops 1077410816 | bytes 6295552 | tf_op jit(solution)/shard_map/dot_general | solution.py:123
  53.8 3.8 %convolution_convert_fusion.1 = bf16[512,1024]{1,0:T(8,128)(2,1)} fusion(bf16[512,1024]{1,0:T(8,128)(2,1)S(1)} %copy-done.15, bf16[1024,1024]{1,0:T(8,128)(2,1)} %all-gather.2.cloned.1.call-done), kind=kOutput, calls=%fused_computation.10 | convolution fusion | flops 1074266112 | bytes 4194304 | tf_op jit(solution)/shard_map/dot_general | solution.py:124
  59.2 2.4 %fusion.22 = f32[16,64,64]{2,1,0:T(8,128)} fusion(bf16[512,16,64]{0,2,1:T(8,128)(2,1)S(1)} %bitcast.74, bf16[512,16,64]{0,2,1:T(8,128)(2,1)} %bitcast.76), kind=kOutput, calls=%fused_computation.70 | convolution fusion | flops 67108864 | bytes 2359296 | tf_op jit(solution)/shard_map/thd,the->dhe/dot_general | solution.py:51
  66.7 3.6 %collective-permute-start.11 = (bf16[65,1024]{1,0:T(8,128)(2,1)}, bf16[65,1024]{1,0:T(8,128)(2,1)}, u32[]{:S(2)}, u32[]{:S(2)}) collective-permute-start(bf16[65,1024]{1,0:T(8,128)(2,1)} %fusion.14), channel_id=1, source_target_pairs={{0,3},{1,4},{2,5},{3,6},{4,7},{5,8},{6,9},{7,10},{8,11},{9,12},{10... | collective-permute-start | bytes 399368 | tf_op jit(solution)/shard_map/ppermute | solution.py:36
  70.3 2.4 %collective-permute-start.10 = (bf16[65,1024]{1,0:T(8,128)(2,1)}, bf16[65,1024]{1,0:T(8,128)(2,1)}, u32[]{:S(2)}, u32[]{:S(2)}) collective-permute-start(bf16[65,1024]{1,0:T(8,128)(2,1)} %fusion.14), channel_id=1, source_target_pairs={{2,0},{3,1},{4,2},{5,3},{6,4},{7,5},{8,6},{9,7},{10,8},{11,9},{12,... | collective-permute-start | bytes 399368 | tf_op jit(solution)/shard_map/ppermute | solution.py:36
  72.8 3.4 %collective-permute-start.9 = (bf16[65,1024]{1,0:T(8,128)(2,1)}, bf16[65,1024]{1,0:T(8,128)(2,1)}, u32[]{:S(2)}, u32[]{:S(2)}) collective-permute-start(bf16[65,1024]{1,0:T(8,128)(2,1)} %fusion.14), channel_id=1, source_target_pairs={{0,2},{1,3},{2,4},{3,5},{4,6},{5,7},{6,8},{7,9},{8,10},{9,11},{10,... | collective-permute-start | bytes 399368 | tf_op jit(solution)/shard_map/ppermute | solution.py:36
  76.2 4.3 %collective-permute-start.8 = (bf16[65,1024]{1,0:T(8,128)(2,1)}, bf16[65,1024]{1,0:T(8,128)(2,1)}, u32[]{:S(2)}, u32[]{:S(2)}) collective-permute-start(bf16[65,1024]{1,0:T(8,128)(2,1)} %fusion.14), channel_id=1, source_target_pairs={{1,0},{2,1},{3,2},{4,3},{5,4},{6,5},{7,6},{8,7},{9,8},{10,9},{11,1... | collective-permute-start | bytes 399368 | tf_op jit(solution)/shard_map/ppermute | solution.py:36
  97.5 2.7 %multiply_reduce_fusion.1 = (f32[128]{0:T(128)S(1)}, f32[128,16,64]{0,2,1:T(8,128)}) fusion(f32[16,64]{1,0:T(8,128)} %mul.100, f32[128,16]{0,1:T(8,128)S(1)} %multiply_reduce_fusion.2, f32[64,16,64]{0,2,1:T(8,128)} %bitcast.85, f32[128,16,64]{0,2,1:T(8,128)} %bitcast.81), kind=kOutput, calls=%fused_computation.22 | convolution fusion | flops 101056384 | bytes 1323520 | tf_op jit(solution)/shard_map/phd,dhe->phe/dot_general | solution.py:80
  105.1 2.9 %fusion.4 = f32[16,64,64]{2,1,0:T(8,128)} fusion(f32[128,16,64]{0,2,1:T(8,128)} %bitcast.82, f32[128]{0:T(128)S(1)} %subtract_reduce_fusion, f32[16,64]{1,0:T(8,128)S(1)} %copy-done.7, f32[128,16]{0,1:T(8,128)S(1)} %multiply_reduce_fusion.2), kind=kOutput, calls=%fused_computation.26 | convolution fusion | flops 100925440 | bytes 799232 | tf_op jit(solution)/shard_map/phd,phe->dhe/dot_general | solution.py:99
  112.3 2.1 %copy.36 = f32[128,1024]{1,0:T(8,128)} copy(f32[128,1024]{0,1:T(8,128)} %bitcast.83) | data formatting | bytes 1048576 | tf_op jit(solution)/shard_map/mul | solution.py:106
  117.0 2.1 %collective-permute-start.18 = (bf16[65,1024]{1,0:T(8,128)(2,1)}, bf16[65,1024]{1,0:T(8,128)(2,1)S(1)}, u32[]{:S(2)}, u32[]{:S(2)}) collective-permute-start(bf16[65,1024]{1,0:T(8,128)(2,1)} %fusion.13), channel_id=1, source_target_pairs={{3,0},{4,1},{5,2},{6,3},{7,4},{8,5},{9,6},{10,7},{11,8},{12,9},{13... | collective-permute-start | bytes 399368 | tf_op jit(solution)/shard_map/ppermute | solution.py:36
  119.1 3.4 %collective-permute-start.17 = (bf16[65,1024]{1,0:T(8,128)(2,1)}, bf16[65,1024]{1,0:T(8,128)(2,1)}, u32[]{:S(2)}, u32[]{:S(2)}) collective-permute-start(bf16[65,1024]{1,0:T(8,128)(2,1)} %fusion.13), channel_id=1, source_target_pairs={{0,3},{1,4},{2,5},{3,6},{4,7},{5,8},{6,9},{7,10},{8,11},{9,12},{10... | collective-permute-start | bytes 399368 | tf_op jit(solution)/shard_map/ppermute | solution.py:36
  122.5 4.2 %collective-permute-start.16 = (bf16[65,1024]{1,0:T(8,128)(2,1)}, bf16[65,1024]{1,0:T(8,128)(2,1)}, u32[]{:S(2)}, u32[]{:S(2)}) collective-permute-start(bf16[65,1024]{1,0:T(8,128)(2,1)} %fusion.13), channel_id=1, source_target_pairs={{2,0},{3,1},{4,2},{5,3},{6,4},{7,5},{8,6},{9,7},{10,8},{11,9},{12,... | collective-permute-start | bytes 399368 | tf_op jit(solution)/shard_map/ppermute | solution.py:36
  128.7 7.4 %collective-permute-start.14 = (bf16[65,1024]{1,0:T(8,128)(2,1)}, bf16[65,1024]{1,0:T(8,128)(2,1)}, u32[]{:S(2)}, u32[]{:S(2)}) collective-permute-start(bf16[65,1024]{1,0:T(8,128)(2,1)} %fusion.13), channel_id=1, source_target_pairs={{1,0},{2,1},{3,2},{4,3},{5,4},{6,5},{7,6},{8,7},{9,8},{10,9},{11,1... | collective-permute-start | bytes 399368 | tf_op jit(solution)/shard_map/ppermute | solution.py:36
  138.2 2.7 %convolution_convert_fusion.2 = bf16[128,1024]{1,0:T(8,128)(2,1)} fusion(bf16[1024,1024]{1,0:T(8,128)(2,1)S(1)} %copy-done, f32[128,1024]{1,0:T(8,128)} %copy.35, f32[128,1024]{1,0:T(8,128)} %get-tuple-element.96), kind=kOutput, calls=%fused_computation.15 | convolution fusion | flops 269221888 | bytes 3407872 | tf_op jit(solution)/shard_map/dot_general | solution.py:109
  143.5 5.9 %collective-permute-done.13 = bf16[65,1024]{1,0:T(8,128)(2,1)S(1)} collective-permute-done((bf16[65,1024]{1,0:T(8,128)(2,1)}, bf16[65,1024]{1,0:T(8,128)(2,1)S(1)}, u32[]{:S(2)}, u32[]{:S(2)}) %collective-permute-start.13) | collective-permute-done | bytes 133152 | tf_op jit(solution)/shard_map/ppermute | solution.py:36
  157.2 3.9 %add_convert_fusion = bf16[512,1024]{1,0:T(8,128)(2,1)} fusion(f32[512,1024]{1,0:T(8,128)S(1)} %fusion.23, bf16[512,1024]{0,1:T(8,128)(2,1)S(1)} %fusion, bf16[1024,1024]{1,0:T(8,128)(2,1)} %constant_dynamic-update-slice_fusion), kind=kOutput, calls=%fused_computation.4 | convolution fusion | flops 1074790400 | bytes 6291456 | tf_op jit(solution)/shard_map/dot_general | solution.py:144
  (105 shorter events, 56.2 us)
Async XLA Ops:
  7.2 10.6 %copy-start.12 = (s32[256,2]{0,1:T(2,128)S(1)}, s32[256,2]{0,1:T(2,128)}, u32[]{:S(2)}) copy-start(s32[256,2]{0,1:T(2,128)} %param.12) | copy-start | bytes 6148
  7.2 46.6 %all-gather.2.cloned.1.call-start = ((), (), s32[]{:S(2)}) async-start(), calls=%async_computation | async-start | bytes 2359296 | tf_op jit(solution)/shard_map/all_gather | solution.py:121
  7.9 14.7 %copy-start.4 = (bf16[128,1024]{1,0:T(8,128)(2,1)S(1)}, bf16[128,1024]{1,0:T(8,128)(2,1)}, u32[]{:S(2)}) copy-start(bf16[128,1024]{1,0:T(8,128)(2,1)} %param.14) | copy-start | bytes 786436
  7.9 10.5 %collective-permute-start.1 = (bf16[128,1024]{1,0:T(8,128)(2,1)}, bf16[128,1024]{1,0:T(8,128)(2,1)S(1)}, u32[]{:S(2)}, u32[]{:S(2)}) collective-permute-start(bf16[128,1024]{1,0:T(8,128)(2,1)} %param.14), channel_id=1, source_target_pairs={{0,7},{1,0},{2,1},{3,2},{4,3},{5,4},{6,5},{7,6},{8,15},{9,8},{10,9... | collective-permute-start | bytes 786440 | tf_op jit(solution)/shard_map/ppermute | solution.py:26
  9.9 7.9 %collective-permute-start = (bf16[128,1024]{1,0:T(8,128)(2,1)}, bf16[128,1024]{1,0:T(8,128)(2,1)S(1)}, u32[]{:S(2)}, u32[]{:S(2)}) collective-permute-start(bf16[128,1024]{1,0:T(8,128)(2,1)} %param.14), channel_id=1, source_target_pairs={{0,1},{1,2},{2,3},{3,4},{4,5},{5,6},{6,7},{7,0},{8,9},{9,10},{10,1... | collective-permute-start | bytes 786440 | tf_op jit(solution)/shard_map/ppermute | solution.py:21
  17.8 11.8 %collective-permute-start.2 = (bf16[128,1024]{1,0:T(8,128)(2,1)S(1)}, bf16[128,1024]{1,0:T(8,128)(2,1)S(1)}, u32[]{:S(2)}, u32[]{:S(2)}) collective-permute-start(bf16[128,1024]{1,0:T(8,128)(2,1)S(1)} %collective-permute-done), channel_id=1, source_target_pairs={{0,1},{1,2},{2,3},{3,4},{4,5},{5,6},{6,7},{7,0},{8,9},{9,10},{10,1... | collective-permute-start | bytes 786440 | tf_op jit(solution)/shard_map/ppermute | solution.py:21
  18.4 12.7 %collective-permute-start.3 = (bf16[128,1024]{1,0:T(8,128)(2,1)S(1)}, bf16[128,1024]{1,0:T(8,128)(2,1)S(1)}, u32[]{:S(2)}, u32[]{:S(2)}) collective-permute-start(bf16[128,1024]{1,0:T(8,128)(2,1)S(1)} %collective-permute-done.1), channel_id=1, source_target_pairs={{0,7},{1,0},{2,1},{3,2},{4,3},{5,4},{6,5},{7,6},{8,15},{9,8},{10,9... | collective-permute-start | bytes 786440 | tf_op jit(solution)/shard_map/ppermute | solution.py:26
  23.4 25.5 %copy-start.14 = (bf16[512,1024]{1,0:T(8,128)(2,1)S(1)}, bf16[512,1024]{1,0:T(8,128)(2,1)}, u32[]{:S(2)}) copy-start(bf16[512,1024]{1,0:T(8,128)(2,1)} %param.10) | copy-start | bytes 3145732
  29.6 11.9 %collective-permute-start.4 = (bf16[128,1024]{1,0:T(8,128)(2,1)S(1)}, bf16[128,1024]{1,0:T(8,128)(2,1)S(1)}, u32[]{:S(2)}, u32[]{:S(2)}) collective-permute-start(bf16[128,1024]{1,0:T(8,128)(2,1)S(1)} %collective-permute-done.2), channel_id=1, source_target_pairs={{0,1},{1,2},{2,3},{3,4},{4,5},{5,6},{6,7},{7,0},{8,9},{9,10},{10,1... | collective-permute-start | bytes 786440 | tf_op jit(solution)/shard_map/ppermute | solution.py:21
  31.1 12.5 %collective-permute-start.5 = (bf16[128,1024]{1,0:T(8,128)(2,1)S(1)}, bf16[128,1024]{1,0:T(8,128)(2,1)S(1)}, u32[]{:S(2)}, u32[]{:S(2)}) collective-permute-start(bf16[128,1024]{1,0:T(8,128)(2,1)S(1)} %collective-permute-done.3), channel_id=1, source_target_pairs={{0,7},{1,0},{2,1},{3,2},{4,3},{5,4},{6,5},{7,6},{8,15},{9,8},{10,9... | collective-permute-start | bytes 786440 | tf_op jit(solution)/shard_map/ppermute | solution.py:26
  41.5 6.7 %collective-permute-start.6 = (bf16[128,1024]{1,0:T(8,128)(2,1)S(1)}, bf16[128,1024]{1,0:T(8,128)(2,1)S(1)}, u32[]{:S(2)}, u32[]{:S(2)}) collective-permute-start(bf16[128,1024]{1,0:T(8,128)(2,1)S(1)} %collective-permute-done.4), channel_id=1, source_target_pairs={{0,1},{1,2},{2,3},{3,4},{4,5},{5,6},{6,7},{7,0},{8,9},{9,10},{10,1... | collective-permute-start | bytes 786440 | tf_op jit(solution)/shard_map/ppermute | solution.py:21
  63.5 17.0 %collective-permute-start.12 = (bf16[65,1024]{1,0:T(8,128)(2,1)}, bf16[65,1024]{1,0:T(8,128)(2,1)S(1)}, u32[]{:S(2)}, u32[]{:S(2)}) collective-permute-start(bf16[65,1024]{1,0:T(8,128)(2,1)} %fusion.14), channel_id=1, source_target_pairs={{3,0},{4,1},{5,2},{6,3},{7,4},{8,5},{9,6},{10,7},{11,8},{12,9},{13... | collective-permute-start | bytes 399368 | tf_op jit(solution)/shard_map/ppermute | solution.py:36
  66.7 27.0 %collective-permute-start.11 = (bf16[65,1024]{1,0:T(8,128)(2,1)}, bf16[65,1024]{1,0:T(8,128)(2,1)}, u32[]{:S(2)}, u32[]{:S(2)}) collective-permute-start(bf16[65,1024]{1,0:T(8,128)(2,1)} %fusion.14), channel_id=1, source_target_pairs={{0,3},{1,4},{2,5},{3,6},{4,7},{5,8},{6,9},{7,10},{8,11},{9,12},{10... | collective-permute-start | bytes 399368 | tf_op jit(solution)/shard_map/ppermute | solution.py:36
  70.3 23.4 %collective-permute-start.10 = (bf16[65,1024]{1,0:T(8,128)(2,1)}, bf16[65,1024]{1,0:T(8,128)(2,1)}, u32[]{:S(2)}, u32[]{:S(2)}) collective-permute-start(bf16[65,1024]{1,0:T(8,128)(2,1)} %fusion.14), channel_id=1, source_target_pairs={{2,0},{3,1},{4,2},{5,3},{6,4},{7,5},{8,6},{9,7},{10,8},{11,9},{12,... | collective-permute-start | bytes 399368 | tf_op jit(solution)/shard_map/ppermute | solution.py:36
  72.8 21.0 %collective-permute-start.9 = (bf16[65,1024]{1,0:T(8,128)(2,1)}, bf16[65,1024]{1,0:T(8,128)(2,1)}, u32[]{:S(2)}, u32[]{:S(2)}) collective-permute-start(bf16[65,1024]{1,0:T(8,128)(2,1)} %fusion.14), channel_id=1, source_target_pairs={{0,2},{1,3},{2,4},{3,5},{4,6},{5,7},{6,8},{7,9},{8,10},{9,11},{10,... | collective-permute-start | bytes 399368 | tf_op jit(solution)/shard_map/ppermute | solution.py:36
  76.2 17.5 %collective-permute-start.8 = (bf16[65,1024]{1,0:T(8,128)(2,1)}, bf16[65,1024]{1,0:T(8,128)(2,1)}, u32[]{:S(2)}, u32[]{:S(2)}) collective-permute-start(bf16[65,1024]{1,0:T(8,128)(2,1)} %fusion.14), channel_id=1, source_target_pairs={{1,0},{2,1},{3,2},{4,3},{5,4},{6,5},{7,6},{8,7},{9,8},{10,9},{11,1... | collective-permute-start | bytes 399368 | tf_op jit(solution)/shard_map/ppermute | solution.py:36
  80.5 13.3 %collective-permute-start.7 = (bf16[65,1024]{1,0:T(8,128)(2,1)}, bf16[65,1024]{1,0:T(8,128)(2,1)}, u32[]{:S(2)}, u32[]{:S(2)}) collective-permute-start(bf16[65,1024]{1,0:T(8,128)(2,1)} %fusion.14), channel_id=1, source_target_pairs={{0,1},{1,2},{2,3},{3,4},{4,5},{5,6},{6,7},{7,8},{8,9},{9,10},{10,1... | collective-permute-start | bytes 399368 | tf_op jit(solution)/shard_map/ppermute | solution.py:36
  117.0 24.0 %collective-permute-start.18 = (bf16[65,1024]{1,0:T(8,128)(2,1)}, bf16[65,1024]{1,0:T(8,128)(2,1)S(1)}, u32[]{:S(2)}, u32[]{:S(2)}) collective-permute-start(bf16[65,1024]{1,0:T(8,128)(2,1)} %fusion.13), channel_id=1, source_target_pairs={{3,0},{4,1},{5,2},{6,3},{7,4},{8,5},{9,6},{10,7},{11,8},{12,9},{13... | collective-permute-start | bytes 399368 | tf_op jit(solution)/shard_map/ppermute | solution.py:36
  119.1 24.4 %collective-permute-start.17 = (bf16[65,1024]{1,0:T(8,128)(2,1)}, bf16[65,1024]{1,0:T(8,128)(2,1)}, u32[]{:S(2)}, u32[]{:S(2)}) collective-permute-start(bf16[65,1024]{1,0:T(8,128)(2,1)} %fusion.13), channel_id=1, source_target_pairs={{0,3},{1,4},{2,5},{3,6},{4,7},{5,8},{6,9},{7,10},{8,11},{9,12},{10... | collective-permute-start | bytes 399368 | tf_op jit(solution)/shard_map/ppermute | solution.py:36
  122.5 20.9 %collective-permute-start.16 = (bf16[65,1024]{1,0:T(8,128)(2,1)}, bf16[65,1024]{1,0:T(8,128)(2,1)}, u32[]{:S(2)}, u32[]{:S(2)}) collective-permute-start(bf16[65,1024]{1,0:T(8,128)(2,1)} %fusion.13), channel_id=1, source_target_pairs={{2,0},{3,1},{4,2},{5,3},{6,4},{7,5},{8,6},{9,7},{10,8},{11,9},{12,... | collective-permute-start | bytes 399368 | tf_op jit(solution)/shard_map/ppermute | solution.py:36
  126.7 16.8 %collective-permute-start.15 = (bf16[65,1024]{1,0:T(8,128)(2,1)}, bf16[65,1024]{1,0:T(8,128)(2,1)}, u32[]{:S(2)}, u32[]{:S(2)}) collective-permute-start(bf16[65,1024]{1,0:T(8,128)(2,1)} %fusion.13), channel_id=1, source_target_pairs={{0,2},{1,3},{2,4},{3,5},{4,6},{5,7},{6,8},{7,9},{8,10},{9,11},{10,... | collective-permute-start | bytes 399368 | tf_op jit(solution)/shard_map/ppermute | solution.py:36
  128.7 14.7 %collective-permute-start.14 = (bf16[65,1024]{1,0:T(8,128)(2,1)}, bf16[65,1024]{1,0:T(8,128)(2,1)}, u32[]{:S(2)}, u32[]{:S(2)}) collective-permute-start(bf16[65,1024]{1,0:T(8,128)(2,1)} %fusion.13), channel_id=1, source_target_pairs={{1,0},{2,1},{3,2},{4,3},{5,4},{6,5},{7,6},{8,7},{9,8},{10,9},{11,1... | collective-permute-start | bytes 399368 | tf_op jit(solution)/shard_map/ppermute | solution.py:36
  138.2 11.2 %copy-start.6 = (f32[1024]{0:T(1024)S(1)}, f32[1024]{0:T(1024)}, u32[]{:S(2)}) copy-start(f32[1024]{0:T(1024)} %copy-done.5) | copy-start | bytes 12292
  141.0 8.5 %collective-permute-start.13 = (bf16[65,1024]{1,0:T(8,128)(2,1)}, bf16[65,1024]{1,0:T(8,128)(2,1)S(1)}, u32[]{:S(2)}, u32[]{:S(2)}) collective-permute-start(bf16[65,1024]{1,0:T(8,128)(2,1)} %fusion.13), channel_id=1, source_target_pairs={{0,1},{1,2},{2,3},{3,4},{4,5},{5,6},{6,7},{7,8},{8,9},{9,10},{10,1... | collective-permute-start | bytes 399368 | tf_op jit(solution)/shard_map/ppermute | solution.py:36
  (12 other events, 53.7 us)
Sparse Core Ops, SparseCore 0:
  9.9 35.2 all-gather.1
